TPU v7x, 512 devices: a whole 4x8x8 slice. The times are simulated.
512 devices in a mesh: shift: 4 (over x_hi, core), space: 128 (over y, z, x_lo).
Axes of the slice: x: 4 (x_hi: 2, x_lo: 2; x = x_hi * 2 + x_lo), y: 8, z: 8, core: 2. Of those that a mesh axis runs over, the one named last changes fastest.
Arguments:
- labels: int32 [256, 32, 256], P('space'), may hold values from 0 to 7
- conductance: float32 [8], replicated, may hold values from 0.2 to 5
- capacity_table: float32 [8], replicated, may hold values from 0.5 to 2
- shift_values: float32 [8], replicated, may hold values from 0.1 to 4
- prior_basis: float32 [256, 256, 32, 256], P(None, 'space', 'shift'), may hold values from -6 to 6
Outputs:
- new_block: float32 [8, 8, 256, 32, 256], P(None, None, 'space', 'shift')
- coefficients: float32 [64, 256], replicated
- factor: float32 [64, 64], replicated
All inputs are finite; a program needn't handle non-finite values.
Results may differ from a plain program's by a relative error of at most 0.0003.
Values sent between devices are 32-bit elements; how exact they have to be, the bound alone decides.
No kernel may reach another device: no remote copies, remote signals or barrier semaphores. Data moves between devices by JAX's collectives and lax.ppermute only.
A program may use at most 64 MiB of HBM per device.

v0:
```python
import jax
import jax.numpy as jnp
from jax import lax
from jax.sharding import PartitionSpec as P

COLS = 8
SWEEPS = 4
LOWER_BOUND = 0.1
UPPER_BOUND = 2.0


def padded_2(cells, sides, width):
    for axis, dim in sides:
        count = lax.axis_size(axis)
        ends = count - 1
        head = lax.slice_in_dim(cells, 0, width, axis=dim)
        tail = lax.slice_in_dim(cells, cells.shape[dim] - width, cells.shape[dim], axis=dim)
        cells = jnp.concatenate(
            [
                lax.ppermute(tail, axis, [(i, (i + 1) % count) for i in range(ends)]),
                cells,
                lax.ppermute(head, axis, [((i + 1) % count, i) for i in range(ends)]),
            ],
            axis=dim,
        )
    return cells


def lookup(labels, table):
    materials = jnp.arange(table.shape[0], dtype=jnp.int32)
    onehot = (labels[None] == materials[:, None, None, None]).astype(jnp.float32)
    return jnp.sum(onehot * table[:, None, None, None], axis=0)


def conductances(conduct, padded):
    west_face = 0.5 * (conduct + padded[:-2, 1:-1, 1:-1])
    east_face = 0.5 * (conduct + padded[2:, 1:-1, 1:-1])
    south_face = 0.5 * (conduct + padded[1:-1, :-2, 1:-1])
    north_face = 0.5 * (conduct + padded[1:-1, 2:, 1:-1])
    below_face = 0.5 * (conduct + padded[1:-1, 1:-1, :-2])
    above_face = 0.5 * (conduct + padded[1:-1, 1:-1, 2:])
    return (west_face, east_face, south_face, north_face, below_face, above_face)


def neighbours(padded, face_list):
    west_face, east_face, south_face, north_face, below_face, above_face = face_list
    summed = west_face * padded[..., :-2, 1:-1, 1:-1] + east_face * padded[..., 2:, 1:-1, 1:-1]
    summed = (
        summed
        + south_face * padded[..., 1:-1, :-2, 1:-1]
        + north_face * padded[..., 1:-1, 2:, 1:-1]
    )
    summed = (
        summed
        + below_face * padded[..., 1:-1, 1:-1, :-2]
        + above_face * padded[..., 1:-1, 1:-1, 2:]
    )
    return summed


def diagonal_of(face_list, shift_list, capacity):
    west_face, east_face, south_face, north_face, below_face, above_face = face_list
    summed = west_face + east_face + (south_face + north_face) + (below_face + above_face)
    return summed[None, None] + shift_list[:, None, None, None, None] * capacity[None, None]


def chebyshev(source, face_list, diagonal, padder):
    center = 0.5 * (UPPER_BOUND + LOWER_BOUND)
    spread = 0.5 * (UPPER_BOUND - LOWER_BOUND)
    ratio_value = center / spread
    reciprocal = 1.0 / diagonal
    solution = jnp.zeros_like(source)
    remainder = source
    weight_old = 1.0 / ratio_value
    direction = reciprocal * remainder / center
    for sweep_index in range(SWEEPS):
        solution = solution + direction
        if sweep_index + 1 < SWEEPS:
            applied = diagonal * direction - neighbours(padder(direction), face_list)
            remainder = remainder - applied
            weight_new = 1.0 / (2.0 * ratio_value - weight_old)
            direction = weight_new * weight_old * direction + 2.0 * weight_new / spread * (
                reciprocal * remainder
            )
            weight_old = weight_new
    return solution


def products(left_side, right_side):
    return lax.dot_general(
        left_side, right_side, (((1,), (1,)), ((), ())), precision=lax.Precision.HIGHEST
    )


def matmul(left_side, right_side):
    return jnp.dot(left_side, right_side, precision=lax.Precision.HIGHEST)


def local(labels, conductance, capacity_table, shift_values, prior_basis):
    groups = lax.axis_size("shift")
    shifts_all = shift_values.shape[0]
    per_device = shifts_all // groups
    new_count = shifts_all * COLS
    basis_count = prior_basis.shape[0]
    slab_x = prior_basis.shape[1]
    quarter = prior_basis.shape[2]
    depth = prior_basis.shape[3]
    flat_basis = prior_basis.reshape(basis_count, slab_x * quarter * depth)
    cell_weight = 1.0 / (slab_x * quarter * depth * groups * lax.axis_size("space"))
    tail_columns = prior_basis[basis_count - new_count :]
    conduct = lookup(labels, conductance)
    capacity = lookup(labels, capacity_table)
    rimmed = padded_2(conduct, (("space", 0),), 1)
    face_list = conductances(conduct, jnp.pad(rimmed, ((0, 0), (1, 1), (1, 1))))
    shift_list = lax.dynamic_slice_in_dim(
        shift_values, lax.axis_index("shift") * per_device, per_device, 0
    )
    diagonal = diagonal_of(face_list, shift_list, capacity)
    starting = lax.all_to_all(tail_columns, "shift", split_axis=0, concat_axis=2, tiled=True)
    full_y = starting.shape[2]
    source = starting.reshape(per_device, COLS, slab_x, full_y, depth) * capacity[None, None]

    def padder(field):
        widened = padded_2(field, (("space", 2),), 1)
        return jnp.pad(widened, ((0, 0), (0, 0), (0, 0), (1, 1), (1, 1)))

    fields = chebyshev(source, face_list, diagonal, padder)
    merged = fields.reshape(per_device * COLS, slab_x, full_y, depth)
    regrouped = lax.all_to_all(merged, "shift", split_axis=2, concat_axis=0, tiled=True)
    columns = regrouped.reshape(new_count, slab_x * quarter * depth)
    first_proj = lax.psum(products(columns, flat_basis), ("shift", "space")) * cell_weight
    columns = columns - matmul(first_proj, flat_basis)
    second_proj = lax.psum(products(columns, flat_basis), ("shift", "space")) * cell_weight
    columns = columns - matmul(second_proj, flat_basis)
    gram_matrix = lax.psum(products(columns, columns), ("shift", "space")) * cell_weight
    factor = jnp.linalg.cholesky(gram_matrix)
    orthonormal = lax.linalg.triangular_solve(factor, columns, left_side=True, lower=True)
    new_block = orthonormal.reshape(shifts_all, COLS, slab_x, quarter, depth)
    return (new_block, first_proj + second_proj, factor)


def solution(mesh):
    in_specs = (P("space", None, None), P(), P(), P(), P(None, "space", "shift", None))
    out_specs = (P(None, None, "space", "shift", None), P(), P())
    return jax.shard_map(local, mesh=mesh, in_specs=in_specs, out_specs=out_specs, check_vma=False)
```

profile of v0, /device:TPU:1, one launch (start us, length us, event | category | flops | bytes accessed | tf_op | source)
XLA Modules:
  0.0 803.1 jit_solution(15233755541338323633)
XLA Ops:
  7.2 2.3 slice.133
  9.5 10.4 %all-to-all-start = ((f32[64,2,8,256]{3,2,1,0:T(8,128)}), f32[64,2,8,256]{3,2,1,0:T(8,128)S(1)}, u32[]{:S(2)}, u32[]{:S(2)}) async-start(f32[64,2,8,256]{3,2,1,0:T(8,128)} %slice.133), calls=%async_computation | async-start | bytes 2097152 | tf_op jit(solution)/shard_map/all_to_all | solution.py:119
  19.9 0.2 select_reduce_fusion.1
  20.1 1.3 collective-permute-start
  21.4 1.3 collective-permute-start.1
  22.7 0.1 dynamic_slice.3
  22.8 10.3 %collective-permute-done = f32[1,32,256]{2,1,0:T(8,128)S(1)} collective-permute-done((f32[1,32,256]{2,1,0:T(8,128)S(1)}, f32[1,32,256]{2,1,0:T(8,128)S(1)}, u32[]{:S(2)}, u32[]{:S(2)}) %collective-permute-start) | collective-permute-done | bytes 32800 | tf_op jit(solution)/shard_map/ppermute | solution.py:20
  33.0 0.0 collective-permute-done.1
  33.0 0.1 select_maximum_fusion.6
  33.2 0.1 add_add_fusion
  33.3 0.1 multiply_add_fusion.2
  33.4 2.3 all-to-all-done
  35.7 0.1 copy.35
  35.8 0.2 fusion.37
  36.0 0.1 fusion.69
  36.1 1.9 collective-permute-start.2
  37.9 1.3 collective-permute-start.3
  39.2 20.6 %collective-permute-done.2 = f32[2,8,1,32,256]{4,3,2,1,0:T(8,128)S(1)} collective-permute-done((f32[2,8,1,32,256]{4,3,2,1,0:T(8,128)S(1)}, f32[2,8,1,32,256]{4,3,2,1,0:T(8,128)S(1)}, u32[]{:S(2)}, u32[]{:S(2)}) %collective-permute-start.2) | collective-permute-done | bytes 524320 | tf_op jit(solution)/shard_map/ppermute | solution.py:20
  59.8 0.0 collective-permute-done.3
  59.8 1.8 select_maximum_fusion.4
  61.6 1.2 multiply_add_fusion.1
  62.8 0.1 fusion.68
  62.9 4.1 collective-permute-start.4
  67.1 1.3 collective-permute-start.5
  68.4 19.6 %collective-permute-done.4 = f32[2,8,1,32,256]{4,3,2,1,0:T(8,128)S(1)} collective-permute-done((f32[2,8,1,32,256]{4,3,2,1,0:T(8,128)S(1)}, f32[2,8,1,32,256]{4,3,2,1,0:T(8,128)S(1)}, u32[]{:S(2)}, u32[]{:S(2)}) %collective-permute-start.4) | collective-permute-done | bytes 524320 | tf_op jit(solution)/shard_map/ppermute | solution.py:20
  88.0 0.0 collective-permute-done.5
  88.0 1.8 select_maximum_fusion.2
  89.8 1.2 multiply_add_fusion
  91.0 0.1 fusion.67
  91.1 4.1 collective-permute-start.6
  95.3 1.3 collective-permute-start.7
  96.6 18.6 %collective-permute-done.6 = f32[2,8,1,32,256]{4,3,2,1,0:T(8,128)S(1)} collective-permute-done((f32[2,8,1,32,256]{4,3,2,1,0:T(8,128)S(1)}, f32[2,8,1,32,256]{4,3,2,1,0:T(8,128)S(1)}, u32[]{:S(2)}, u32[]{:S(2)}) %collective-permute-start.6) | collective-permute-done | bytes 524320 | tf_op jit(solution)/shard_map/ppermute | solution.py:20
  115.1 0.0 collective-permute-done.7
  115.1 1.8 select_maximum_fusion
  117.0 1.4 fusion.9
  118.3 1.8 copy.36
  120.1 6.9 all-to-all-start.1
  127.0 0.0 all-reduce.7.cloned.1.call-start
  127.0 7.9 copy.46
  135.0 7.2 all-to-all-done.1
  142.1 0.6 copy.53
  142.8 0.1 copy.38
  142.9 0.2 reshape.60
  143.1 6.8 fusion.71
  149.9 0.0 all-reduce.7.cloned.1.call-update
  149.9 0.3 all-reduce.9.cloned.1.call-start
  150.2 267.6 %all-reduce.7.cloned.1.call-done = f32[64,256]{1,0:T(8,128)} async-done(((f32[64,256]{1,0:T(8,128)}), f32[64,256]{1,0:T(8,128)}) %all-reduce.7.cloned.1.call-update) | async-done | bytes 65552 | tf_op jit(solution)/shard_map/psum | solution.py:131
  417.8 5.0 convolution_subtract_fusion.1
  422.7 4.6 fusion.72
  427.3 0.0 all-reduce.9.cloned.1.call-update
  427.4 251.4 %all-reduce.9.cloned.1.call-done = f32[64,256]{1,0:T(8,128)} async-done(((f32[64,256]{1,0:T(8,128)}), f32[64,256]{1,0:T(8,128)}) %all-reduce.9.cloned.1.call-update) | async-done | bytes 65552 | tf_op jit(solution)/shard_map/psum | solution.py:133
  678.8 4.8 convolution_subtract_fusion
  683.6 1.0 fusion.73
  684.6 94.9 %psum.23 = f32[64,64]{0,1:T(8,128)S(1)} all-reduce(f32[64,64]{0,1:T(8,128)S(1)} %fusion.73), channel_id=1, replica_groups=mesh['shift'=4,'space'=128] {'shift','space'}, use_global_device_ids=true, to_apply=%region_4.5 | all-reduce | flops 4096 | bytes 32768 | tf_op jit(solution)/shard_map/psum | solution.py:135
  779.5 0.1 copy.40
  779.6 5.8 cholesky.16
  785.5 0.6 compare_reduce_fusion
  786.1 1.3 select_bitcast_fusion
  787.4 4.9 custom-call.6
  792.3 0.1 copy.41
  792.4 0.3 copy.47
  792.7 1.6 fusion.34
  794.3 1.3 copy.43
  795.6 0.6 multiply_add_fusion.3
  (18 shorter events, 0.1 us)
Async XLA Ops:
  7.2 12.7 %copy-start.5 = (f32[8]{0:T(128)S(1)}, f32[8]{0:T(128)}, u32[]{:S(2)}) copy-start(f32[8]{0:T(128)} %param.7) | copy-start | bytes 100
  7.2 12.7 %copy-start.4 = (f32[8]{0:T(128)S(1)}, f32[8]{0:T(128)}, u32[]{:S(2)}) copy-start(f32[8]{0:T(128)} %param.6) | copy-start | bytes 100
  7.2 12.7 %copy-start.3 = (s32[2,32,256]{2,1,0:T(8,128)S(1)}, s32[2,32,256]{2,1,0:T(8,128)}, u32[]{:S(2)}) copy-start(s32[2,32,256]{2,1,0:T(8,128)} %param.5) | copy-start | bytes 196612
  7.2 15.5 %copy-start.6 = (f32[8]{0:T(128)S(1)}, f32[8]{0:T(128)}, u32[]{:S(2)}) copy-start(f32[8]{0:T(128)} %param.8) | copy-start | bytes 100
  9.5 26.2 %all-to-all-start = ((f32[64,2,8,256]{3,2,1,0:T(8,128)}), f32[64,2,8,256]{3,2,1,0:T(8,128)S(1)}, u32[]{:S(2)}, u32[]{:S(2)}) async-start(f32[64,2,8,256]{3,2,1,0:T(8,128)} %slice.133), calls=%async_computation | async-start | bytes 2097152 | tf_op jit(solution)/shard_map/all_to_all | solution.py:119
  20.1 13.0 %collective-permute-start = (f32[1,32,256]{2,1,0:T(8,128)S(1)}, f32[1,32,256]{2,1,0:T(8,128)S(1)}, u32[]{:S(2)}, u32[]{:S(2)}) collective-permute-start(f32[1,32,256]{2,1,0:T(8,128)S(1)} %get-tuple-element.42), channel_id=1, source_target_pairs={{0,1},{1,2},{2,3},{3,4},{4,5},{5,6},{6,7},{7,8},{8,9},{9,10},{10,1... | collective-permute-start | bytes 98312 | tf_op jit(solution)/shard_map/ppermute | solution.py:20
  21.4 11.7 %collective-permute-start.1 = (f32[1,32,256]{2,1,0:T(8,128)S(1)}, f32[1,32,256]{2,1,0:T(8,128)S(1)}, u32[]{:S(2)}, u32[]{:S(2)}) collective-permute-start(f32[1,32,256]{2,1,0:T(8,128)S(1)} %get-tuple-element.43), channel_id=1, source_target_pairs={{1,0},{2,1},{3,2},{4,3},{5,4},{6,5},{7,6},{8,7},{9,8},{10,9},{11,1... | collective-permute-start | bytes 98312 | tf_op jit(solution)/shard_map/ppermute | solution.py:22
  36.1 23.7 %collective-permute-start.2 = (f32[2,8,1,32,256]{4,3,2,1,0:T(8,128)S(1)}, f32[2,8,1,32,256]{4,3,2,1,0:T(8,128)S(1)}, u32[]{:S(2)}, u32[]{:S(2)}) collective-permute-start(f32[2,8,1,32,256]{4,3,2,1,0:T(8,128)S(1)} %get-tuple-element.37), channel_id=1, source_target_pairs={{0,1},{1,2},{2,3},{3,4},{4,5},{5,6},{6,7},{7,8},{8,9},{9,10},{10,1... | collective-permute-start | bytes 1572872 | tf_op jit(solution)/shard_map/ppermute | solution.py:20
  37.9 21.9 %collective-permute-start.3 = (f32[2,8,1,32,256]{4,3,2,1,0:T(8,128)S(1)}, f32[2,8,1,32,256]{4,3,2,1,0:T(8,128)S(1)}, u32[]{:S(2)}, u32[]{:S(2)}) collective-permute-start(f32[2,8,1,32,256]{4,3,2,1,0:T(8,128)S(1)} %get-tuple-element.38), channel_id=1, source_target_pairs={{1,0},{2,1},{3,2},{4,3},{5,4},{6,5},{7,6},{8,7},{9,8},{10,9},{11,1... | collective-permute-start | bytes 1572872 | tf_op jit(solution)/shard_map/ppermute | solution.py:22
  62.9 25.1 %collective-permute-start.4 = (f32[2,8,1,32,256]{4,3,2,1,0:T(8,128)S(1)}, f32[2,8,1,32,256]{4,3,2,1,0:T(8,128)S(1)}, u32[]{:S(2)}, u32[]{:S(2)}) collective-permute-start(f32[2,8,1,32,256]{4,3,2,1,0:T(8,128)S(1)} %get-tuple-element.35), channel_id=1, source_target_pairs={{0,1},{1,2},{2,3},{3,4},{4,5},{5,6},{6,7},{7,8},{8,9},{9,10},{10,1... | collective-permute-start | bytes 1572872 | tf_op jit(solution)/shard_map/ppermute | solution.py:20
  67.1 20.9 %collective-permute-start.5 = (f32[2,8,1,32,256]{4,3,2,1,0:T(8,128)S(1)}, f32[2,8,1,32,256]{4,3,2,1,0:T(8,128)S(1)}, u32[]{:S(2)}, u32[]{:S(2)}) collective-permute-start(f32[2,8,1,32,256]{4,3,2,1,0:T(8,128)S(1)} %get-tuple-element.36), channel_id=1, source_target_pairs={{1,0},{2,1},{3,2},{4,3},{5,4},{6,5},{7,6},{8,7},{9,8},{10,9},{11,1... | collective-permute-start | bytes 1572872 | tf_op jit(solution)/shard_map/ppermute | solution.py:22
  91.1 24.0 %collective-permute-start.6 = (f32[2,8,1,32,256]{4,3,2,1,0:T(8,128)S(1)}, f32[2,8,1,32,256]{4,3,2,1,0:T(8,128)S(1)}, u32[]{:S(2)}, u32[]{:S(2)}) collective-permute-start(f32[2,8,1,32,256]{4,3,2,1,0:T(8,128)S(1)} %get-tuple-element.33), channel_id=1, source_target_pairs={{0,1},{1,2},{2,3},{3,4},{4,5},{5,6},{6,7},{7,8},{8,9},{9,10},{10,1... | collective-permute-start | bytes 1572872 | tf_op jit(solution)/shard_map/ppermute | solution.py:20
  95.3 19.9 %collective-permute-start.7 = (f32[2,8,1,32,256]{4,3,2,1,0:T(8,128)S(1)}, f32[2,8,1,32,256]{4,3,2,1,0:T(8,128)S(1)}, u32[]{:S(2)}, u32[]{:S(2)}) collective-permute-start(f32[2,8,1,32,256]{4,3,2,1,0:T(8,128)S(1)} %get-tuple-element.34), channel_id=1, source_target_pairs={{1,0},{2,1},{3,2},{4,3},{5,4},{6,5},{7,6},{8,7},{9,8},{10,9},{11,1... | collective-permute-start | bytes 1572872 | tf_op jit(solution)/shard_map/ppermute | solution.py:22
  120.1 22.0 %all-to-all-start.1 = ((f32[16,2,32,256]{3,1,0,2:T(2,128)}), f32[16,2,32,256]{3,1,0,2:T(2,128)S(1)}, u32[]{:S(2)}, u32[]{:S(2)}) async-start(f32[16,2,32,256]{3,1,0,2:T(2,128)} %copy.36), calls=%async_computation.1 | async-start | bytes 2097152 | tf_op jit(solution)/shard_map/all_to_all | solution.py:129
  127.0 290.7 %all-reduce.7.cloned.1.call-start = ((), (), s32[]{:S(2)}) async-start(), calls=%async_computation.2 | async-start | bytes 131072 | tf_op jit(solution)/shard_map/psum | solution.py:131
  149.9 528.9 %all-reduce.9.cloned.1.call-start = ((), (), s32[]{:S(2)}) async-start(), calls=%async_computation.3 | async-start | bytes 131072 | tf_op jit(solution)/shard_map/psum | solution.py:133
  417.8 5.0 copy-start
  684.6 111.0 %copy-start.1 = (f32[64,256]{1,0:T(8,128)S(1)}, f32[64,256]{1,0:T(8,128)}, u32[]{:S(2)}) copy-start(f32[64,256]{1,0:T(8,128)} %all-reduce.7.cloned.1.call-done) | copy-start | bytes 196612
  684.6 111.0 %copy-start.2 = (f32[64,256]{1,0:T(8,128)S(1)}, f32[64,256]{1,0:T(8,128)}, u32[]{:S(2)}) copy-start(f32[64,256]{1,0:T(8,128)} %all-reduce.9.cloned.1.call-done) | copy-start | bytes 196612
Sparse Core Ops, SparseCore 0:
  150.0 267.6 all-reduce.6
  427.5 251.2 all-reduce.8
where the time goes:
time: 804 us; the launch traced here: 803 us
  waiting for transfers between devices  598 us (74%)
  blocking collectives  94.9 us (12%)
  starting transfers between devices  34.2 us (4%)
  matrix products  23.7 us (3%)
  other arithmetic  23.2 us (3%)
  local copies, waits for them, and re-layouts  15.2 us (2%)
  between operations  14.3 us (2%)
    psum x2, waiting for transfers between devices, local(): lax.psum(products(columns, flat_basis), ('shift', 'space')) * cell_weight  519 us
    psum x1, blocking collectives, local(): lax.psum(products(columns, columns), ('shift', 'space')) * cell_weight  94.9 us
    ppermute x4, waiting for transfers between devices, padded_2(): lax.ppermute(tail, axis, [(i, (i + 1) % count) for i in range(ends)])  69 us
  transfers between devices with their start and end apart: 12, of which 8 were waited for; matrix products, arithmetic and copies ran while one was open for 1% of the time, Pallas kernels for 0%

commit v1 on v0

--- a/solution.py
+++ b/solution.py
@@ -128,7 +128,7 @@
     merged = fields.reshape(per_device * COLS, slab_x, full_y, depth)
     regrouped = lax.all_to_all(merged, "shift", split_axis=2, concat_axis=0, tiled=True)
     columns = regrouped.reshape(new_count, slab_x * quarter * depth)
-    first_proj = lax.psum(products(columns, flat_basis), ("shift", "space")) * cell_weight
+    first_proj = lax.psum(lax.psum(products(columns, flat_basis), "shift"), "space") * cell_weight
     columns = columns - matmul(first_proj, flat_basis)
     second_proj = lax.psum(products(columns, flat_basis), ("shift", "space")) * cell_weight
     columns = columns - matmul(second_proj, flat_basis)

time: 804 us -> 1630 us (2.03)
  waiting for transfers between devices: 598 us -> 1430 us
    psum x0 -> x2, waiting for transfers between devices: none -> 1040 us  [the longest x1 978 us: local(): lax.psum(lax.psum(products(columns, flat_basis), 'shift'), 'space')]
    psum x2 -> x1, waiting for transfers between devices: 519 us -> 313 us  [local(): lax.psum(products(columns, flat_basis), ('shift', 'space')) * cell_weight]
  transfers between devices with their start and end apart: 12 -> 13, of which waited for: 8 -> 9; matrix products, arithmetic and copies ran while one was open for 1% -> 1% of each run, Pallas kernels for 0% -> 0%
where the time goes in v1:
time: 1630 us
  waiting for transfers between devices  1430 us (88%)
  blocking collectives  94.9 us (6%)
  starting transfers between devices  34.2 us (2%)
  matrix products  23.7 us (1%)
  other arithmetic  23.2 us (1%)
    psum x1, waiting for transfers between devices, local(): lax.psum(lax.psum(products(columns, flat_basis), 'shift'), 'space')  978 us
    psum x1, waiting for transfers between devices, local(): lax.psum(products(columns, flat_basis), ('shift', 'space')) * cell_weight  313 us
    psum x1, blocking collectives, local(): lax.psum(products(columns, columns), ('shift', 'space')) * cell_weight  94.9 us
    ppermute x4, waiting for transfers between devices, padded_2(): lax.ppermute(tail, axis, [(i, (i + 1) % count) for i in range(ends)])  69 us
    psum x1, waiting for transfers between devices, local(): lax.psum(products(columns, flat_basis), 'shift')  59.8 us
  transfers between devices with their start and end apart: 13, of which 9 were waited for; matrix products, arithmetic and copies ran while one was open for 1% of the time, Pallas kernels for 0%

profile of v1, /device:TPU:1, one launch (start us, length us, event | category | flops | bytes accessed | tf_op | source)
XLA Modules:
  0.0 1633.9 jit_solution(6214768572337846708)
XLA Ops:
  7.2 2.3 slice.133
  9.5 10.4 all-to-all-start
  19.9 0.2 select_reduce_fusion.1
  20.1 1.3 collective-permute-start
  21.4 1.3 collective-permute-start.1
  22.7 0.1 dynamic_slice.3
  22.8 10.3 collective-permute-done
  33.0 0.0 collective-permute-done.1
  33.0 0.1 select_maximum_fusion.6
  33.2 0.1 add_add_fusion
  33.3 0.1 multiply_add_fusion.2
  33.4 2.3 all-to-all-done
  35.7 0.1 copy.35
  35.8 0.2 fusion.37
  36.0 0.1 fusion.69
  36.1 1.9 collective-permute-start.2
  37.9 1.3 collective-permute-start.3
  39.2 20.6 %collective-permute-done.2 = f32[2,8,1,32,256]{4,3,2,1,0:T(8,128)S(1)} collective-permute-done((f32[2,8,1,32,256]{4,3,2,1,0:T(8,128)S(1)}, f32[2,8,1,32,256]{4,3,2,1,0:T(8,128)S(1)}, u32[]{:S(2)}, u32[]{:S(2)}) %collective-permute-start.2) | collective-permute-done | bytes 524320 | tf_op jit(solution)/shard_map/ppermute | solution.py:20
  59.8 0.0 collective-permute-done.3
  59.8 1.8 select_maximum_fusion.4
  61.6 1.2 multiply_add_fusion.1
  62.8 0.1 fusion.68
  62.9 4.1 collective-permute-start.4
  67.1 1.3 collective-permute-start.5
  68.4 19.6 %collective-permute-done.4 = f32[2,8,1,32,256]{4,3,2,1,0:T(8,128)S(1)} collective-permute-done((f32[2,8,1,32,256]{4,3,2,1,0:T(8,128)S(1)}, f32[2,8,1,32,256]{4,3,2,1,0:T(8,128)S(1)}, u32[]{:S(2)}, u32[]{:S(2)}) %collective-permute-start.4) | collective-permute-done | bytes 524320 | tf_op jit(solution)/shard_map/ppermute | solution.py:20
  88.0 1.8 select_maximum_fusion.2
  89.8 1.2 multiply_add_fusion
  91.0 0.1 fusion.67
  91.1 4.1 collective-permute-start.6
  95.3 1.3 collective-permute-start.7
  96.6 18.6 %collective-permute-done.6 = f32[2,8,1,32,256]{4,3,2,1,0:T(8,128)S(1)} collective-permute-done((f32[2,8,1,32,256]{4,3,2,1,0:T(8,128)S(1)}, f32[2,8,1,32,256]{4,3,2,1,0:T(8,128)S(1)}, u32[]{:S(2)}, u32[]{:S(2)}) %collective-permute-start.6) | collective-permute-done | bytes 524320 | tf_op jit(solution)/shard_map/ppermute | solution.py:20
  115.1 1.8 select_maximum_fusion
  117.0 1.4 fusion.9
  118.3 1.8 copy.36
  120.1 6.9 all-to-all-start.1
  127.0 7.9 copy.46
  135.0 7.2 all-to-all-done.1
  142.1 0.6 copy.53
  142.8 0.1 copy.38
  142.9 0.2 reshape.60
  143.1 6.8 fusion.71
  149.9 0.0 all-reduce.8.cloned.1.call-update
  149.9 0.0 all-reduce.10.cloned.1.call-start
  149.9 59.8 %all-reduce.8.cloned.1.call-done = f32[64,256]{1,0:T(8,128)} async-done(((f32[64,256]{1,0:T(8,128)}), f32[64,256]{1,0:T(8,128)}) %all-reduce.8.cloned.1.call-update) | async-done | bytes 65552 | tf_op jit(solution)/shard_map/psum | solution.py:131
  209.7 0.0 all-reduce.10.cloned.1.call-update
  209.8 0.3 all-reduce.12.cloned.1.call-start
  210.0 977.7 %all-reduce.10.cloned.1.call-done = f32[64,256]{1,0:T(8,128)} async-done(((f32[64,256]{1,0:T(8,128)}), f32[64,256]{1,0:T(8,128)}) %all-reduce.10.cloned.1.call-update) | async-done | bytes 65552 | tf_op jit(solution)/shard_map/psum | solution.py:131
  1187.8 5.0 convolution_subtract_fusion.1
  1192.8 4.6 fusion.72
  1197.4 0.0 all-reduce.12.cloned.1.call-update
  1197.4 312.5 %all-reduce.12.cloned.1.call-done = f32[64,256]{1,0:T(8,128)} async-done(((f32[64,256]{1,0:T(8,128)}), f32[64,256]{1,0:T(8,128)}) %all-reduce.12.cloned.1.call-update) | async-done | bytes 65552 | tf_op jit(solution)/shard_map/psum | solution.py:133
  1509.9 4.8 convolution_subtract_fusion
  1514.7 1.0 fusion.73
  1515.7 94.9 %psum.31 = f32[64,64]{0,1:T(8,128)S(1)} all-reduce(f32[64,64]{0,1:T(8,128)S(1)} %fusion.73), channel_id=1, replica_groups=mesh['shift'=4,'space'=128] {'shift','space'}, use_global_device_ids=true, to_apply=%region_5.6 | all-reduce | flops 4096 | bytes 32768 | tf_op jit(solution)/shard_map/psum | solution.py:135
  1610.6 0.1 copy.40
  1610.7 5.8 cholesky.16
  1616.6 0.6 compare_reduce_fusion
  1617.2 1.3 select_bitcast_fusion
  1618.5 4.9 custom-call.6
  1623.4 0.1 copy.41
  1623.5 0.3 copy.47
  1623.8 1.6 fusion.34
  1625.4 1.3 copy.43
  1626.7 0.6 multiply_add_fusion.3
  (21 shorter events, 0.1 us)
Async XLA Ops:
  7.2 12.7 copy-start.5
  7.2 12.7 copy-start.4
  7.2 12.7 copy-start.3
  7.2 15.5 copy-start.6
  9.5 26.2 %all-to-all-start = ((f32[64,2,8,256]{3,2,1,0:T(8,128)}), f32[64,2,8,256]{3,2,1,0:T(8,128)S(1)}, u32[]{:S(2)}, u32[]{:S(2)}) async-start(f32[64,2,8,256]{3,2,1,0:T(8,128)} %slice.133), calls=%async_computation | async-start | bytes 2097152 | tf_op jit(solution)/shard_map/all_to_all | solution.py:119
  20.1 13.0 collective-permute-start
  21.4 11.7 collective-permute-start.1
  36.1 23.7 %collective-permute-start.2 = (f32[2,8,1,32,256]{4,3,2,1,0:T(8,128)S(1)}, f32[2,8,1,32,256]{4,3,2,1,0:T(8,128)S(1)}, u32[]{:S(2)}, u32[]{:S(2)}) collective-permute-start(f32[2,8,1,32,256]{4,3,2,1,0:T(8,128)S(1)} %get-tuple-element.37), channel_id=1, source_target_pairs={{0,1},{1,2},{2,3},{3,4},{4,5},{5,6},{6,7},{7,8},{8,9},{9,10},{10,1... | collective-permute-start | bytes 1572872 | tf_op jit(solution)/shard_map/ppermute | solution.py:20
  37.9 21.9 %collective-permute-start.3 = (f32[2,8,1,32,256]{4,3,2,1,0:T(8,128)S(1)}, f32[2,8,1,32,256]{4,3,2,1,0:T(8,128)S(1)}, u32[]{:S(2)}, u32[]{:S(2)}) collective-permute-start(f32[2,8,1,32,256]{4,3,2,1,0:T(8,128)S(1)} %get-tuple-element.38), channel_id=1, source_target_pairs={{1,0},{2,1},{3,2},{4,3},{5,4},{6,5},{7,6},{8,7},{9,8},{10,9},{11,1... | collective-permute-start | bytes 1572872 | tf_op jit(solution)/shard_map/ppermute | solution.py:22
  62.9 25.1 %collective-permute-start.4 = (f32[2,8,1,32,256]{4,3,2,1,0:T(8,128)S(1)}, f32[2,8,1,32,256]{4,3,2,1,0:T(8,128)S(1)}, u32[]{:S(2)}, u32[]{:S(2)}) collective-permute-start(f32[2,8,1,32,256]{4,3,2,1,0:T(8,128)S(1)} %get-tuple-element.35), channel_id=1, source_target_pairs={{0,1},{1,2},{2,3},{3,4},{4,5},{5,6},{6,7},{7,8},{8,9},{9,10},{10,1... | collective-permute-start | bytes 1572872 | tf_op jit(solution)/shard_map/ppermute | solution.py:20
  67.1 20.9 %collective-permute-start.5 = (f32[2,8,1,32,256]{4,3,2,1,0:T(8,128)S(1)}, f32[2,8,1,32,256]{4,3,2,1,0:T(8,128)S(1)}, u32[]{:S(2)}, u32[]{:S(2)}) collective-permute-start(f32[2,8,1,32,256]{4,3,2,1,0:T(8,128)S(1)} %get-tuple-element.36), channel_id=1, source_target_pairs={{1,0},{2,1},{3,2},{4,3},{5,4},{6,5},{7,6},{8,7},{9,8},{10,9},{11,1... | collective-permute-start | bytes 1572872 | tf_op jit(solution)/shard_map/ppermute | solution.py:22
  91.1 24.0 %collective-permute-start.6 = (f32[2,8,1,32,256]{4,3,2,1,0:T(8,128)S(1)}, f32[2,8,1,32,256]{4,3,2,1,0:T(8,128)S(1)}, u32[]{:S(2)}, u32[]{:S(2)}) collective-permute-start(f32[2,8,1,32,256]{4,3,2,1,0:T(8,128)S(1)} %get-tuple-element.33), channel_id=1, source_target_pairs={{0,1},{1,2},{2,3},{3,4},{4,5},{5,6},{6,7},{7,8},{8,9},{9,10},{10,1... | collective-permute-start | bytes 1572872 | tf_op jit(solution)/shard_map/ppermute | solution.py:20
  95.3 19.9 %collective-permute-start.7 = (f32[2,8,1,32,256]{4,3,2,1,0:T(8,128)S(1)}, f32[2,8,1,32,256]{4,3,2,1,0:T(8,128)S(1)}, u32[]{:S(2)}, u32[]{:S(2)}) collective-permute-start(f32[2,8,1,32,256]{4,3,2,1,0:T(8,128)S(1)} %get-tuple-element.34), channel_id=1, source_target_pairs={{1,0},{2,1},{3,2},{4,3},{5,4},{6,5},{7,6},{8,7},{9,8},{10,9},{11,1... | collective-permute-start | bytes 1572872 | tf_op jit(solution)/shard_map/ppermute | solution.py:22
  120.1 22.0 %all-to-all-start.1 = ((f32[16,2,32,256]{3,1,0,2:T(2,128)}), f32[16,2,32,256]{3,1,0,2:T(2,128)S(1)}, u32[]{:S(2)}, u32[]{:S(2)}) async-start(f32[16,2,32,256]{3,1,0,2:T(2,128)} %copy.36), calls=%async_computation.1 | async-start | bytes 2097152 | tf_op jit(solution)/shard_map/all_to_all | solution.py:129
  127.0 82.7 %all-reduce.8.cloned.1.call-start = ((), (), s32[]{:S(2)}) async-start(), calls=%async_computation.2 | async-start | bytes 131072 | tf_op jit(solution)/shard_map/psum | solution.py:131
  149.9 1037.9 %all-reduce.10.cloned.1.call-start = ((), (), s32[]{:S(2)}) async-start(), calls=%async_computation.3 | async-start | bytes 131072 | tf_op jit(solution)/shard_map/psum | solution.py:131
  209.8 1300.1 %all-reduce.12.cloned.1.call-start = ((), (), s32[]{:S(2)}) async-start(), calls=%async_computation.4 | async-start | bytes 131072 | tf_op jit(solution)/shard_map/psum | solution.py:133
  1187.8 5.0 copy-start
  1515.7 111.0 %copy-start.1 = (f32[64,256]{1,0:T(8,128)S(1)}, f32[64,256]{1,0:T(8,128)}, u32[]{:S(2)}) copy-start(f32[64,256]{1,0:T(8,128)} %all-reduce.10.cloned.1.call-done) | copy-start | bytes 196612
  1515.7 111.0 %copy-start.2 = (f32[64,256]{1,0:T(8,128)S(1)}, f32[64,256]{1,0:T(8,128)}, u32[]{:S(2)}) copy-start(f32[64,256]{1,0:T(8,128)} %all-reduce.12.cloned.1.call-done) | copy-start | bytes 196612
Sparse Core Ops, SparseCore 0:
  150.0 59.6 all-reduce.7
  212.9 974.8 all-reduce.9
  1197.5 312.3 all-reduce.11
